TPU v7x, 32 devices: a whole 2x2x4 slice. The times are simulated.
32 devices in a mesh: ctx: 8 (over y, x, core), head: 4 (over z).
Axes of the slice: x: 2, y: 2, z: 4, core: 2. Of those that a mesh axis runs over, the one named last changes fastest.
Arguments:
- query_rows: bfloat16 [6144, 4096], P('ctx', 'head'), may hold values from -6 to 6
- key_rows: bfloat16 [6144, 4096], P('ctx', 'head'), may hold values from -3.5 to 3.5
- value_rows: bfloat16 [6144, 4096], P('ctx', 'head'), may hold values from -6 to 6
- cluster_ids: int32 [32, 6144, 1], P('head', 'ctx'), may hold values from 0 to 255; in each aligned block of 768 rows (0 to 767, 768 to 1535, ..., all dimensions but the last counted through in order) at most 6 rows name the same one
- centroids: float32 [32, 256, 128], P('head', 'ctx'), may hold values from -6 to 6
- out_weight: bfloat16 [4096, 4096], P(None, 'head'), may hold values from -0.09375 to 0.09375
Outputs:
- layer_output: bfloat16 [6144, 4096], P('ctx', 'head')
- new_centroids: float32 [32, 256, 128], P('head', 'ctx')
Inputs may be any that keep to these rules, and one draw needn't show every extreme that they name: `cluster_ids`: in each aligned block of 768 tokens of one head (the tokens of one index of ctx), no cluster is named by more than 6 tokens, a bound that some block reaches.
All inputs are finite; a program needn't handle non-finite values.
Results may differ from a plain program's by a relative error of at most 0.014.
Values may be sent and summed in bfloat16 or wider, within the bound.
No kernel may reach another device: no remote copies, remote signals or barrier semaphores. Data moves between devices by JAX's collectives and lax.ppermute only.
A program may use at most 128 MiB of HBM per device.

v0:
```python
import jax
import jax.numpy as jnp
from jax import lax
from jax.sharding import PartitionSpec as P

CLUSTERS = 256


prior_weight = 64.0


def slot_targets(labels, per_owner, slot_count):
    length = labels.shape[0]
    order_ids = jnp.arange(length, dtype=jnp.int32)
    same_label = labels[:, None] == labels[None, :]
    earlier = order_ids[None, :] < order_ids[:, None]
    token_rank = jnp.sum((same_label & earlier).astype(jnp.int32), axis=1)
    owner_of = labels // per_owner
    local_of = labels % per_owner
    return owner_of * (slot_count * per_owner) + token_rank * per_owner + local_of


def slot_matrix(targets, row_total):
    return jnp.arange(row_total, dtype=jnp.int32)[:, None] == targets[None, :]


def attend_blocks(query_blk, key_blk, value_blk, place_blk, per_owner):
    heads_here, sources, width_slots, head_dim = query_blk.shape
    row_count = sources * width_slots // per_owner
    query_view = query_blk.reshape(heads_here, row_count, per_owner, head_dim)
    key_view = key_blk.reshape(heads_here, row_count, per_owner, head_dim)
    value_view = value_blk.reshape(heads_here, row_count, per_owner, head_dim)
    place_view = jnp.transpose(place_blk.reshape(heads_here, row_count, per_owner), (0, 2, 1))
    scores = jnp.einsum(
        "hicd,hjcd->hcij", query_view, key_view, preferred_element_type=jnp.float32
    ) * head_dim ** (-0.5)
    allowed = (place_view[:, :, None, :] >= 0) & (
        place_view[:, :, None, :] <= place_view[:, :, :, None]
    )
    scores = jnp.where(allowed, scores, jnp.float32(-1e30))
    top_score = jnp.max(scores, axis=3, keepdims=True)
    weights = jnp.exp(scores - top_score)
    totals = jnp.sum(weights, axis=3, keepdims=True)
    attention_weights = (weights / totals).astype(jnp.bfloat16)
    result = jnp.einsum(
        "hcij,hjcd->hicd", attention_weights, value_view, preferred_element_type=jnp.float32
    ).astype(jnp.bfloat16)
    return result.reshape(heads_here, sources, width_slots, head_dim)


def sent_sums(key_buf, place_buf, slot_count, per_owner):
    heads_here, ctx_count, width_slots, head_dim = key_buf.shape
    key_view = key_buf.reshape(heads_here, ctx_count, slot_count, per_owner, head_dim)
    local_totals = jnp.sum(key_view, axis=2, dtype=jnp.float32).reshape(
        heads_here, ctx_count * per_owner, head_dim
    )
    place_view = (
        (place_buf >= 0).reshape(heads_here, ctx_count, slot_count, per_owner).astype(jnp.float32)
    )
    local_counts = jnp.sum(place_view, axis=2).reshape(heads_here, ctx_count * per_owner)
    return (local_totals, local_counts)


def local(query_rows, key_rows, value_rows, cluster_ids, centroids, out_weight):
    ctx_count = lax.axis_size("ctx")
    token_count = query_rows.shape[0]
    heads_here = cluster_ids.shape[0]
    head_dim = query_rows.shape[1] // heads_here
    clusters = CLUSTERS
    per_owner = clusters // ctx_count
    slot_count = 2 * token_count // clusters
    row_total = clusters * slot_count
    labels = cluster_ids[:, :, 0]
    first_position = lax.axis_index("ctx") * token_count
    token_ids = jnp.arange(token_count, dtype=jnp.int32)
    stacked = jnp.concatenate(
        (
            query_rows.reshape(token_count, heads_here, head_dim),
            key_rows.reshape(token_count, heads_here, head_dim),
            value_rows.reshape(token_count, heads_here, head_dim),
        ),
        axis=2,
    )
    stacked = jnp.transpose(stacked, (1, 0, 2))

    def dispatch_head(inputs):
        head_labels, head_rows = inputs
        targets = slot_targets(head_labels, per_owner, slot_count)
        selector = slot_matrix(targets, row_total)
        filled = jnp.dot(
            selector.astype(jnp.bfloat16), head_rows, preferred_element_type=jnp.float32
        ).astype(jnp.bfloat16)
        token_at = jnp.max(jnp.where(selector, token_ids[None, :], -1), axis=1)
        place = jnp.where(token_at >= 0, first_position + token_at, -1)
        return (filled, place, targets)

    filled_all, place_all, targets_all = lax.map(dispatch_head, (labels, stacked))
    buffer_shape = (heads_here, ctx_count, slot_count * per_owner, head_dim)
    query_buf = filled_all[:, :, :head_dim].reshape(buffer_shape)
    key_buf = filled_all[:, :, head_dim : 2 * head_dim].reshape(buffer_shape)
    value_buf = filled_all[:, :, 2 * head_dim :].reshape(buffer_shape)
    place_buf = place_all.reshape(heads_here, ctx_count, slot_count * per_owner)
    outgoing = (query_buf, key_buf, value_buf, place_buf)
    received = (
        lax.all_to_all(outgoing[0], "ctx", split_axis=1, concat_axis=1, tiled=True),
        lax.all_to_all(outgoing[1], "ctx", split_axis=1, concat_axis=1, tiled=True),
        lax.all_to_all(outgoing[2], "ctx", split_axis=1, concat_axis=1, tiled=True),
        lax.all_to_all(outgoing[3], "ctx", split_axis=1, concat_axis=1, tiled=True),
    )
    result = attend_blocks(received[0], received[1], received[2], received[3], per_owner)
    returned = lax.all_to_all(result, "ctx", split_axis=1, concat_axis=1, tiled=True)
    local_totals, local_counts = sent_sums(key_buf, place_buf, slot_count, per_owner)
    whole_totals, whole_counts = (
        lax.psum(local_totals.astype(jnp.bfloat16), "ctx").astype(jnp.float32),
        lax.psum(local_counts.astype(jnp.bfloat16), "ctx").astype(jnp.float32),
    )
    offset = lax.axis_index("ctx") * per_owner
    totals = lax.dynamic_slice_in_dim(whole_totals, offset, per_owner, 1)
    counts = lax.dynamic_slice_in_dim(whole_counts, offset, per_owner, 1)
    new_centroids = (prior_weight * centroids + totals) / (prior_weight + counts[:, :, None])
    returned_flat = returned.reshape(heads_here, row_total, head_dim)

    def collect_head(inputs):
        targets, head_result = inputs
        selector = slot_matrix(targets, row_total).astype(jnp.bfloat16)
        gathered = lax.dot_general(
            selector, head_result, (((0,), (0,)), ((), ())), preferred_element_type=jnp.float32
        )
        return gathered.astype(jnp.bfloat16)

    per_head = lax.map(collect_head, (targets_all, returned_flat))
    attended = jnp.transpose(per_head, (1, 0, 2)).reshape(token_count, heads_here * head_dim)
    mixed_total = jnp.dot(
        lax.all_gather(attended, "head", axis=1, tiled=True),
        out_weight,
        preferred_element_type=jnp.float32,
    )
    return (mixed_total.astype(jnp.bfloat16), new_centroids)


def solution(mesh):
    placed = (
        P("ctx", "head"),
        P("ctx", "head"),
        P("ctx", "head"),
        P("head", "ctx", None),
        P("head", "ctx", None),
        P(None, "head"),
    )
    return jax.shard_map(
        local,
        mesh=mesh,
        in_specs=placed,
        out_specs=(P("ctx", "head"), P("head", "ctx", None)),
        check_vma=False,
    )
```

profile of v0, /device:TPU:0, one launch (start us, length us, event | category | flops | bytes accessed | tf_op | source)
XLA Modules:
  0.0 422.4 jit_solution(17267256723173437781)
XLA Ops:
  11.5 2.6 copy.88
  14.1 3.5 maximum_bitcast_fusion
  17.6 49.7 %while.30 = (s32[]{:T(128)}, bf16[8,1536,384]{2,1,0:T(8,128)(2,1)}, s32[8,1536]{1,0:T(8,128)S(1)}, s32[8,768]{1,0:T(8,128)}, s32[8,768]{1,0:T(8,128)S(1)}, /*index=5*/bf16[8,768,384]{1,2,0:T(8,128)(2,1)}, s32[]{:T(128)}) while((s32[]{:T(128)}, bf16[8,1536,384]{2,1,0:T(8,128)(2,1)}, s32[8,1536]{1,0:T(8,128)S(1)}, ...), condition=%wide.region_3.4_spmd.clone.clone, body=%wide.region_0.3_spmd.clone.sunk.clone | while | flops 914247168 | bytes 1856609 | solution.py:97
  18.0 3.5 fusion.67
  24.2 3.5 fusion.67
  30.5 3.5 fusion.67
  36.7 3.5 fusion.67
  42.9 3.5 fusion.67
  49.1 3.5 fusion.67
  55.3 3.5 fusion.67
  61.5 3.6 fusion.67
  68.1 5.2 %all-to-all-start.1 = ((s32[8,8,192]{2,0,1:T(8,128)}), s32[8,8,192]{2,0,1:T(8,128)S(1)}, u32[]{:S(2)}, u32[]{:S(2)}) async-start(s32[8,8,192]{2,0,1:T(8,128)} %copy.92), calls=%async_computation.1 | async-start | bytes 131072 | tf_op jit(solution)/shard_map/all_to_all | solution.py:108
  73.2 5.8 %fusion.39 = (bf16[8,1536,128]{2,1,0:T(8,128)(2,1)}, bf16[8,1536,128]{2,1,0:T(8,128)(2,1)}, bf16[8,1536,128]{2,1,0:T(8,128)(2,1)S(1)}) fusion(bf16[8,1536,384]{2,1,0:T(8,128)(2,1)} %get-tuple-element.131), kind=kLoop, calls=%fused_computation.61 | loop fusion | bytes 18874368 | tf_op jit(solution)/shard_map/slice | solution.py:101
  81.0 4.4 %all-to-all-start.3 = ((bf16[8,8,192,128]{3,2,0,1:T(8,128)(2,1)}), bf16[8,8,192,128]{3,2,0,1:T(8,128)(2,1)}, u32[]{:S(2)}, u32[]{:S(2)}) async-start(bf16[8,8,192,128]{3,2,0,1:T(8,128)(2,1)} %copy.97), calls=%async_computation.3 | async-start | bytes 6291456 | tf_op jit(solution)/shard_map/all_to_all | solution.py:106
  85.5 3.8 copy.95
  89.3 34.1 %all-to-all-done.3 = bf16[8,8,192,128]{3,2,0,1:T(8,128)(2,1)} async-done(((bf16[8,8,192,128]{3,2,0,1:T(8,128)(2,1)}), bf16[8,8,192,128]{3,2,0,1:T(8,128)(2,1)}, u32[]{:S(2)}, u32[]{:S(2)}) %all-to-all-start.3) | async-done | bytes 3145760 | tf_op jit(solution)/shard_map/all_to_all | solution.py:106
  123.4 4.4 %all-to-all-start.2 = ((bf16[8,8,192,128]{3,2,0,1:T(8,128)(2,1)}), bf16[8,8,192,128]{3,2,0,1:T(8,128)(2,1)}, u32[]{:S(2)}, u32[]{:S(2)}) async-start(bf16[8,8,192,128]{3,2,0,1:T(8,128)(2,1)} %copy.95), calls=%async_computation.2 | async-start | bytes 6291456 | tf_op jit(solution)/shard_map/all_to_all | solution.py:105
  127.8 3.9 copy.90
  131.7 34.0 %all-to-all-done.2 = bf16[8,8,192,128]{3,2,0,1:T(8,128)(2,1)} async-done(((bf16[8,8,192,128]{3,2,0,1:T(8,128)(2,1)}), bf16[8,8,192,128]{3,2,0,1:T(8,128)(2,1)}, u32[]{:S(2)}, u32[]{:S(2)}) %all-to-all-start.2) | async-done | bytes 3145760 | tf_op jit(solution)/shard_map/all_to_all | solution.py:105
  165.7 4.4 %all-to-all-start = ((bf16[8,8,192,128]{3,2,0,1:T(8,128)(2,1)}), bf16[8,8,192,128]{3,2,0,1:T(8,128)(2,1)}, u32[]{:S(2)}, u32[]{:S(2)}) async-start(bf16[8,8,192,128]{3,2,0,1:T(8,128)(2,1)} %copy.90), calls=%async_computation | async-start | bytes 6291456 | tf_op jit(solution)/shard_map/all_to_all | solution.py:107
  170.5 3.8 copy.98
  174.3 3.8 copy.96
  178.1 10.1 %fusion.40 = (f32[8,32,48]{2,1,0:T(8,128)S(1)}, f32[8,32,48,48]{2,3,1,0:T(8,128)}) fusion(s32[8,32,48]{2,1,0:T(8,128)S(1)} %bitcast.66, pred[8,32,48]{2,1,0:T(8,128)(4,1)S(1)} %broadcast_compare_fusion, bf16[8,48,32,128]{3,2,1,0:T(8,128)(2,1)} %bitcast.61, bf16[8,48,32,128]{3,2,1,0:T(8,128)(2,1)} %bitcast.62), kind=kOutput, calls=%fused_computation.62 | convolution fusion | flops 154533936 | bytes 8761344 | tf_op jit(solution)/shard_map/sub | solution.py:42
  188.3 19.8 %all-to-all-done = bf16[8,8,192,128]{3,2,0,1:T(8,128)(2,1)} async-done(((bf16[8,8,192,128]{3,2,0,1:T(8,128)(2,1)}), bf16[8,8,192,128]{3,2,0,1:T(8,128)(2,1)}, u32[]{:S(2)}, u32[]{:S(2)}) %all-to-all-start) | async-done | bytes 3145760 | tf_op jit(solution)/shard_map/all_to_all | solution.py:107
  208.1 2.2 copy.91
  216.6 4.4 %all-to-all-start.4 = ((bf16[8,8,192,128]{3,2,0,1:T(8,128)(2,1)}), bf16[8,8,192,128]{3,2,0,1:T(8,128)(2,1)}, u32[]{:S(2)}, u32[]{:S(2)}) async-start(bf16[8,8,192,128]{3,2,0,1:T(8,128)(2,1)} %copy.104), calls=%async_computation.4 | async-start | bytes 6291456 | tf_op jit(solution)/shard_map/all_to_all | solution.py:111
  223.0 38.1 %all-to-all-done.4 = bf16[8,8,192,128]{3,2,0,1:T(8,128)(2,1)} async-done(((bf16[8,8,192,128]{3,2,0,1:T(8,128)(2,1)}), bf16[8,8,192,128]{3,2,0,1:T(8,128)(2,1)}, u32[]{:S(2)}, u32[]{:S(2)}) %all-to-all-start.4) | async-done | bytes 3145760 | tf_op jit(solution)/shard_map/all_to_all | solution.py:111
  261.2 2.2 copy.105
  263.4 24.2 %while.29 = (s32[]{:T(128)}, bf16[8,768,128]{1,2,0:T(8,128)(2,1)}, s32[8,768]{1,0:T(8,128)}, bf16[8,1536,128]{2,1,0:T(8,128)(2,1)S(1)}) while((s32[]{:T(128)}, bf16[8,768,128]{1,2,0:T(8,128)(2,1)}, s32[8,768]{1,0:T(8,128)}, bf16[8,1536,128]{2,1,0:T(8,128)(2,1)S(1)}) %tuple.74), condition=%wide.region_7.8_spmd.clone, body=%wide.region_6.7_spmd.sunk.clone | while | flops 303267840 | bytes 1387069 | solution.py:131
  288.7 11.8 %psum.15 = bf16[8,256]{1,0:T(8,128)(2,1)S(1)} all-reduce(bf16[8,256]{1,0:T(8,128)(2,1)S(1)} %convert_element_type.71), channel_id=1, replica_groups=mesh['ctx'=8,'head'=4] {'ctx'}, use_global_device_ids=true, to_apply=%region_11.12 | all-reduce | flops 2048 | bytes 8192 | tf_op jit(solution)/shard_map/psum | solution.py:115
  302.2 100.6 %all-gather.2.cloned.1.call-done = bf16[768,4096]{0,1:T(8,128)(2,1)} async-done(((bf16[768,1024]{0,1:T(8,128)(2,1)}), bf16[768,4096]{0,1:T(8,128)(2,1)}) %all-gather.2.cloned.1.call-update) | async-done | bytes 6291472 | tf_op jit(solution)/shard_map/all_gather | solution.py:134
  402.9 12.1 %convolution_convert_fusion = bf16[768,1024]{1,0:T(8,128)(2,1)} fusion(bf16[768,4096]{0,1:T(8,128)(2,1)} %all-gather.2.cloned.1.call-done, bf16[4096,1024]{1,0:T(8,128)(2,1)} %param.15), kind=kOutput, calls=%fused_computation.52 | convolution fusion | flops 6443237376 | bytes 16252928 | tf_op jit(solution)/shard_map/dot_general | solution.py:133
  (140 shorter events, 62.9 us)
Async XLA Ops:
  9.8 4.3 %copy-start.1 = (s32[8,768,1]{1,2,0:T(1,128)S(1)}, s32[8,768,1]{1,2,0:T(1,128)}, u32[]{:S(2)}) copy-start(s32[8,768,1]{1,2,0:T(1,128)} %param.13) | copy-start | bytes 73732
  67.3 0.7 copy-start
  68.1 13.0 %all-to-all-start.1 = ((s32[8,8,192]{2,0,1:T(8,128)}), s32[8,8,192]{2,0,1:T(8,128)S(1)}, u32[]{:S(2)}, u32[]{:S(2)}) async-start(s32[8,8,192]{2,0,1:T(8,128)} %copy.92), calls=%async_computation.1 | async-start | bytes 131072 | tf_op jit(solution)/shard_map/all_to_all | solution.py:108
  81.0 42.3 %all-to-all-start.3 = ((bf16[8,8,192,128]{3,2,0,1:T(8,128)(2,1)}), bf16[8,8,192,128]{3,2,0,1:T(8,128)(2,1)}, u32[]{:S(2)}, u32[]{:S(2)}) async-start(bf16[8,8,192,128]{3,2,0,1:T(8,128)(2,1)} %copy.97), calls=%async_computation.3 | async-start | bytes 6291456 | tf_op jit(solution)/shard_map/all_to_all | solution.py:106
  123.4 42.3 %all-to-all-start.2 = ((bf16[8,8,192,128]{3,2,0,1:T(8,128)(2,1)}), bf16[8,8,192,128]{3,2,0,1:T(8,128)(2,1)}, u32[]{:S(2)}, u32[]{:S(2)}) async-start(bf16[8,8,192,128]{3,2,0,1:T(8,128)(2,1)} %copy.95), calls=%async_computation.2 | async-start | bytes 6291456 | tf_op jit(solution)/shard_map/all_to_all | solution.py:105
  165.7 42.3 %all-to-all-start = ((bf16[8,8,192,128]{3,2,0,1:T(8,128)(2,1)}), bf16[8,8,192,128]{3,2,0,1:T(8,128)(2,1)}, u32[]{:S(2)}, u32[]{:S(2)}) async-start(bf16[8,8,192,128]{3,2,0,1:T(8,128)(2,1)} %copy.90), calls=%async_computation | async-start | bytes 6291456 | tf_op jit(solution)/shard_map/all_to_all | solution.py:107
  208.1 3.7 copy-start.2
  216.6 44.6 %all-to-all-start.4 = ((bf16[8,8,192,128]{3,2,0,1:T(8,128)(2,1)}), bf16[8,8,192,128]{3,2,0,1:T(8,128)(2,1)}, u32[]{:S(2)}, u32[]{:S(2)}) async-start(bf16[8,8,192,128]{3,2,0,1:T(8,128)(2,1)} %copy.104), calls=%async_computation.4 | async-start | bytes 6291456 | tf_op jit(solution)/shard_map/all_to_all | solution.py:111
  221.1 79.5 %all-reduce.2.cloned.1.call-start = ((), (), s32[]{:S(2)}) async-start(), calls=%async_computation.6 | async-start | bytes 1048576 | tf_op jit(solution)/shard_map/psum | solution.py:114
  222.8 180.1 %all-gather.2.cloned.1.call-start = ((), (), s32[]{:S(2)}) async-start(), calls=%async_computation.5 | async-start | bytes 7864320 | tf_op jit(solution)/shard_map/all_gather | solution.py:134
Sparse Core Ops, SparseCore 0:
  225.0 66.7 all-reduce.1
Sparse Core Ops, SparseCore 1:
  287.7 115.1 all-gather.1
where the time goes:
time: 425 us; the launch traced here: 422 us
  waiting for transfers between devices  227 us (53%)
  local copies, waits for them, and re-layouts  64.1 us (15%)
  matrix products  63.6 us (15%)
  starting transfers between devices  23.2 us (5%)
  other arithmetic  16.8 us (4%)
  between operations  15.6 us (4%)
  blocking collectives  11.8 us (3%)
    all_gather x1, waiting for transfers between devices, local(): lax.all_gather(attended, 'head', axis=1, tiled=True)  101 us
    all_to_all x1, waiting for transfers between devices, local(): lax.all_to_all(result, 'ctx', split_axis=1, concat_axis=1, tiled=True)  38.1 us
    all_to_all x1, waiting for transfers between devices, local(): lax.all_to_all(outgoing[1], 'ctx', split_axis=1, concat_axis=1, tiled=True)  34.1 us
    all_to_all x1, waiting for transfers between devices, local(): lax.all_to_all(outgoing[0], 'ctx', split_axis=1, concat_axis=1, tiled=True)  34 us
    dot_general x8, matrix products, dispatch_head(): jnp.dot(selector.astype(jnp.bfloat16), head_rows, preferred_element_type=...  28.1 us
    all_to_all x1, waiting for transfers between devices, local(): lax.all_to_all(outgoing[2], 'ctx', split_axis=1, concat_axis=1, tiled=True)  19.8 us
    dynamic_update_slice x16, local copies, waits for them, and re-layouts, local(): lax.map(dispatch_head, (labels, stacked))  12.2 us
    dot_general x1, matrix products, local(): jnp.dot(lax.all_gather(attended, 'head', axis=1, tiled=True), out_weight,...  12.1 us
  transfers between devices with their start and end apart: 7, of which 5 were waited for; matrix products, arithmetic and copies ran while one was open for 15% of the time, Pallas kernels for 0%

commit v1 on v0

v1 whole, which is shorter than its diff:
```python
import jax
import jax.numpy as jnp
from jax import lax
from jax.sharding import PartitionSpec as P

CLUSTERS = 256


prior_weight = 64.0


def slot_targets(labels, per_owner, slot_count):
    length = labels.shape[1]
    order_ids = jnp.arange(length, dtype=jnp.int32)
    same_label = labels[:, :, None] == labels[:, None, :]
    earlier = order_ids[None, :] < order_ids[:, None]
    token_rank = jnp.sum((same_label & earlier[None]).astype(jnp.int32), axis=2)
    owner_of = labels // per_owner
    local_of = labels % per_owner
    return owner_of * (slot_count * per_owner) + token_rank * per_owner + local_of


def attend_blocks(recv, counts_recv, per_owner, head_dim):
    heads_here, sources, width_slots, _ = recv.shape
    slot_count = width_slots // per_owner
    row_count = sources * slot_count
    view = recv.reshape(heads_here, row_count, per_owner, 3 * head_dim)
    query_view = view[..., :head_dim]
    key_view = view[..., head_dim : 2 * head_dim]
    value_view = view[..., 2 * head_dim :]
    rank_ids = jnp.arange(slot_count, dtype=jnp.int32)
    valid = rank_ids[None, None, :, None] < counts_recv[:, :, None, :]
    valid = jnp.transpose(valid.reshape(heads_here, row_count, per_owner), (0, 2, 1))
    row_ids = jnp.arange(row_count, dtype=jnp.int32)
    causal = row_ids[None, :] <= row_ids[:, None]
    allowed = valid[:, :, None, :] & causal[None, None]
    scores = jnp.einsum(
        "hicd,hjcd->hcij", query_view, key_view, preferred_element_type=jnp.float32
    ) * head_dim ** (-0.5)
    scores = jnp.where(allowed, scores, jnp.float32(-1e30))
    top_score = jnp.max(scores, axis=3, keepdims=True)
    weights = jnp.exp(scores - top_score)
    totals = jnp.sum(weights, axis=3, keepdims=True)
    attention_weights = (weights / totals).astype(jnp.bfloat16)
    result = jnp.einsum(
        "hcij,hjcd->hicd", attention_weights, value_view, preferred_element_type=jnp.float32
    ).astype(jnp.bfloat16)
    key_sums = jnp.sum(key_view.astype(jnp.float32), axis=1)
    key_counts = jnp.sum(counts_recv, axis=1).astype(jnp.float32)
    return result.reshape(heads_here, sources, width_slots, head_dim), key_sums, key_counts


def local(query_rows, key_rows, value_rows, cluster_ids, centroids, out_weight):
    ctx_count = lax.axis_size("ctx")
    token_count = query_rows.shape[0]
    heads_here = cluster_ids.shape[0]
    head_dim = query_rows.shape[1] // heads_here
    clusters = CLUSTERS
    per_owner = clusters // ctx_count
    slot_count = 2 * token_count // clusters
    row_total = clusters * slot_count
    labels = cluster_ids[:, :, 0]
    targets = slot_targets(labels, per_owner, slot_count)
    head_ids = jnp.arange(heads_here, dtype=jnp.int32)
    token_ids = jnp.arange(token_count, dtype=jnp.int32)
    token_at = jnp.full((heads_here, row_total), token_count, jnp.int32)
    token_at = token_at.at[head_ids[:, None], targets].set(
        jnp.broadcast_to(token_ids[None, :], targets.shape), unique_indices=True
    )
    filled_slot = token_at < token_count
    flat_index = jnp.where(filled_slot, token_at * heads_here + head_ids[:, None], 0)

    def pick(rows):
        table = rows.reshape(token_count * heads_here, head_dim)
        got = jnp.take(table, flat_index, axis=0)
        return jnp.where(filled_slot[..., None], got, jnp.zeros_like(got))

    send = jnp.concatenate(
        (pick(query_rows), pick(key_rows), pick(value_rows)), axis=2
    ).reshape(heads_here, ctx_count, slot_count * per_owner, 3 * head_dim)
    one_hot = labels[:, :, None] == jnp.arange(clusters, dtype=jnp.int32)[None, None, :]
    counts_send = jnp.sum(one_hot.astype(jnp.int32), axis=1).reshape(
        heads_here, ctx_count, per_owner
    )
    recv = lax.all_to_all(send, "ctx", split_axis=1, concat_axis=1, tiled=True)
    counts_recv = lax.all_to_all(counts_send, "ctx", split_axis=1, concat_axis=1, tiled=True)
    result, key_sums, key_counts = attend_blocks(recv, counts_recv, per_owner, head_dim)
    new_centroids = (prior_weight * centroids + key_sums) / (prior_weight + key_counts[:, :, None])
    returned = lax.all_to_all(result, "ctx", split_axis=1, concat_axis=1, tiled=True)
    returned_flat = returned.reshape(heads_here * row_total, head_dim)
    back_index = jnp.transpose(targets + head_ids[:, None] * row_total, (1, 0))
    attended = jnp.take(returned_flat, back_index, axis=0).reshape(
        token_count, heads_here * head_dim
    )
    mixed_total = jnp.dot(
        lax.all_gather(attended, "head", axis=1, tiled=True),
        out_weight,
        preferred_element_type=jnp.float32,
    )
    return (mixed_total.astype(jnp.bfloat16), new_centroids)


def solution(mesh):
    placed = (
        P("ctx", "head"),
        P("ctx", "head"),
        P("ctx", "head"),
        P("head", "ctx", None),
        P("head", "ctx", None),
        P(None, "head"),
    )
    return jax.shard_map(
        local,
        mesh=mesh,
        in_specs=placed,
        out_specs=(P("ctx", "head"), P("head", "ctx", None)),
        check_vma=False,
    )
```

time: 425 us -> 541 us (1.27)
  local copies, waits for them, and re-layouts: 64.1 us -> 213 us
  matrix products: 63.6 us -> 16.4 us
  waiting for transfers between devices: 227 us -> 252 us
  other arithmetic: 16.8 us -> 28.9 us
  blocking collectives: 11.8 us -> 0 us
  starting transfers between devices: 23.2 us -> 15.2 us
    gather x0 -> x4, local copies, waits for them, and re-layouts: none -> 152 us  [the longest x3 130 us: pick(): got = jnp.take(table, flat_index, axis=0)]
    dot_general x16 -> x1, matrix products: 39.4 us -> 2.14 us  [attend_blocks(): jnp.einsum('hicd,hjcd->hcij', query_view, key_view, preferred_element_typ...]
    unnamed x10 -> x16, local copies, waits for them, and re-layouts: 7.51 us -> 26.9 us
    dynamic_update_slice x32 -> x0, local copies, waits for them, and re-layouts: 18.9 us -> none  [the longest x16 12.2 us: local(): lax.map(dispatch_head, (labels, stacked))]
    all_to_all x4 -> x2, waiting for transfers between devices: 87.9 us -> 104 us  [the longest x1 104 us: local(): recv = lax.all_to_all(send, 'ctx', split_axis=1, concat_axis=1, tiled=True)]
    psum x1 -> x0, blocking collectives: 11.8 us -> none  [local(): lax.psum(local_counts.astype(jnp.bfloat16), 'ctx').astype(jnp.float32)]
    all_gather x1, waiting for transfers between devices: 101 us -> 112 us  [local(): lax.all_gather(attended, 'head', axis=1, tiled=True)]
    sub x1 -> x0, matrix products: 10.1 us -> none  [attend_blocks(): weights = jnp.exp(scores - top_score)]
  transfers between devices with their start and end apart: 7 -> 4, of which waited for: 5 -> 3; matrix products, arithmetic and copies ran while one was open for 15% -> 35% of each run, Pallas kernels for 0% -> 0%
where the time goes in v1:
time: 541 us; the launch traced here: 540 us
  waiting for transfers between devices  252 us (47%)
  local copies, waits for them, and re-layouts  213 us (39%)
  other arithmetic  28.9 us (5%)
  matrix products  16.4 us (3%)
  starting transfers between devices  15.2 us (3%)
  between operations  14.4 us (3%)
    gather x3, local copies, waits for them, and re-layouts, pick(): got = jnp.take(table, flat_index, axis=0)  130 us
    all_gather x1, waiting for transfers between devices, local(): lax.all_gather(attended, 'head', axis=1, tiled=True)  112 us
    all_to_all x1, waiting for transfers between devices, local(): recv = lax.all_to_all(send, 'ctx', split_axis=1, concat_axis=1, tiled=True)  104 us
    all_to_all x1, waiting for transfers between devices, local(): lax.all_to_all(result, 'ctx', split_axis=1, concat_axis=1, tiled=True)  36.9 us
    unnamed x16, local copies, waits for them, and re-layouts  26.9 us
    gather x1, local copies, waits for them, and re-layouts, local(): jnp.take(returned_flat, back_index, axis=0)  22.3 us
    dot_general x1, matrix products, local(): jnp.dot(lax.all_gather(attended, 'head', axis=1, tiled=True), out_weight,...  12 us
  transfers between devices with their start and end apart: 4, of which 3 were waited for; matrix products, arithmetic and copies ran while one was open for 35% of the time, Pallas kernels for 0%

profile of v1, /device:TPU:0, one launch (start us, length us, event | category | flops | bytes accessed | tf_op | source)
XLA Modules:
  0.0 540.2 jit_solution(5230525954035740918)
XLA Ops:
  7.9 1.2 convert_reduce_fusion.2
  9.8 5.2 all-to-all-start.1
  15.2 4.4 convert_reduce_fusion
  19.6 0.8 compare_select_fusion.1
  21.9 23.0 %scatter_custom_fusion = s32[12288]{0:T(1024)S(1)} fusion(s32[6144]{0:T(1024)S(1)} %reshape.145, s32[6144]{0:T(1024)S(1)} %reshape.147, s32[]{:T(128)} %constant.74.clone.1), kind=kCustom, calls=%fused_computation.63 | custom fusion | bytes 49156
  45.1 2.6 reshape.97
  47.6 2.6 reshape.98
  50.2 43.3 %gather_fusion.1 = bf16[12288,128]{1,0:T(8,128)(2,1)} fusion(bf16[6144,128]{1,0:T(8,128)(2,1)S(1)} %reshape.97, s32[12288]{0:T(1024)S(1)} %broadcast_clamp_fusion), kind=kCustom, calls=%fused_computation.clone | custom fusion | bytes 6340608 | tf_op jit(solution)/shard_map/jit(_take)/gather | solution.py:75
  93.5 43.3 %gather_fusion.2 = bf16[12288,128]{1,0:T(8,128)(2,1)} fusion(bf16[6144,128]{1,0:T(8,128)(2,1)S(1)} %reshape.98, s32[12288]{0:T(1024)S(1)} %broadcast_clamp_fusion), kind=kCustom, calls=%fused_computation.1.clone | custom fusion | bytes 6340608 | tf_op jit(solution)/shard_map/jit(_take)/gather | solution.py:75
  137.5 43.3 %gather_fusion.3 = bf16[12288,128]{1,0:T(8,128)(2,1)} fusion(bf16[6144,128]{1,0:T(8,128)(2,1)S(1)} %reshape.99, s32[12288]{0:T(1024)S(1)} %broadcast_clamp_fusion), kind=kCustom, calls=%fused_computation.2.clone | custom fusion | bytes 6340608 | tf_op jit(solution)/shard_map/jit(_take)/gather | solution.py:75
  180.8 6.5 %select_select_fusion.2 = (bf16[8,1536,128]{2,1,0:T(8,128)(2,1)S(1)}, bf16[8,1536,128]{2,1,0:T(8,128)(2,1)S(1)}, bf16[8,1536,128]{2,1,0:T(8,128)(2,1)S(1)}) fusion(bf16[8,1536,128]{2,1,0:T(8,128)(2,1)} %bitcast.43, pred[8,1536]{1,0:T(8,128)(4,1)S(1)} %get-tuple-element.5, pred[8,1536]{1,0:T(8,128)(4,1)S(1)} %reshape.110, bf16[8,1536,128]{2,1,0:T(8,128)(2,1)} %bitcast.44, ...), kind=kLoop, calls=%fused_computation.21 | loop fusion | flops 9437184 | bytes 18898944 | tf_op jit(solution)/shard_map/jit(_where)/select_n | solution.py:76
  187.3 4.7 pad_maximum_fusion
  191.9 8.6 %copy.49 = bf16[8,8,192,384]{3,2,0,1:T(8,128)(2,1)} copy(bf16[8,8,192,384]{3,2,1,0:T(8,128)(2,1)} %bitcast.41) | data formatting | bytes 18874368 | tf_op jit(solution)/shard_map/reshape | solution.py:80
  200.5 5.2 all-to-all-start
  207.4 103.8 %all-to-all-done = bf16[8,8,192,384]{3,2,0,1:T(8,128)(2,1)} async-done(((bf16[8,8,192,384]{3,2,0,1:T(8,128)(2,1)}), bf16[8,8,192,384]{3,2,0,1:T(8,128)(2,1)}, u32[]{:S(2)}, u32[]{:S(2)}) %all-to-all-start) | async-done | bytes 9437216 | tf_op jit(solution)/shard_map/all_to_all | solution.py:85
  311.2 8.6 %copy.50 = bf16[8,8,192,384]{3,2,1,0:T(8,128)(2,1)} copy(bf16[8,8,192,384]{3,2,0,1:T(8,128)(2,1)} %all-to-all-done) | data formatting | bytes 18874368 | tf_op jit(solution)/shard_map/all_to_all | solution.py:85
  319.8 4.6 fusion.34
  324.4 2.1 fusion.3
  326.5 3.5 fusion.35
  330.0 2.2 convert_bitcast_fusion
  332.2 0.8 copy.57
  333.0 2.0 copy.58
  335.0 4.6 all-to-all-start.2
  340.6 36.9 %all-to-all-done.2 = bf16[8,8,192,128]{3,2,0,1:T(8,128)(2,1)} async-done(((bf16[8,8,192,128]{3,2,0,1:T(8,128)(2,1)}), bf16[8,8,192,128]{3,2,0,1:T(8,128)(2,1)}, u32[]{:S(2)}, u32[]{:S(2)}) %all-to-all-start.2) | async-done | bytes 3145760 | tf_op jit(solution)/shard_map/all_to_all | solution.py:89
  377.4 2.2 copy.59
  379.6 22.3 %gather_fusion = bf16[6144,128]{1,0:T(8,128)(2,1)} fusion(bf16[12288,128]{1,0:T(8,128)(2,1)S(1)} %bitcast.39, s32[6144]{0:T(1024)S(1)} %broadcast_clamp_fusion.1), kind=kCustom, calls=%fused_computation.3 | custom fusion | bytes 3170304 | tf_op jit(solution)/shard_map/jit(_take)/gather | solution.py:92
  401.9 2.9 bitcast_select_fusion
  404.8 1.6 copy.83
  406.4 0.8 copy-done.1
  407.2 1.8 convert_reduce_fusion.1
  409.7 111.5 %all-gather.2.cloned.1.call-done = bf16[768,4096]{1,0:T(8,128)(2,1)} async-done(((bf16[768,1024]{1,0:T(8,128)(2,1)}), bf16[768,4096]{1,0:T(8,128)(2,1)}) %all-gather.2.cloned.1.call-update) | async-done | bytes 6291472 | tf_op jit(solution)/shard_map/all_gather | solution.py:96
  521.3 12.0 %convolution_convert_fusion = bf16[768,1024]{1,0:T(8,128)(2,1)} fusion(bf16[768,4096]{1,0:T(8,128)(2,1)} %all-gather.2.cloned.1.call-done, bf16[4096,1024]{1,0:T(8,128)(2,1)} %param.13), kind=kOutput, calls=%fused_computation.30 | convolution fusion | flops 6443237376 | bytes 16252928 | tf_op jit(solution)/shard_map/dot_general | solution.py:95
  (49 shorter events, 7.4 us)
Async XLA Ops:
  9.8 190.7 %all-to-all-start.1 = ((s32[8,1,256]{2,1,0:T(1,128)}), s32[8,1,256]{2,1,0:T(1,128)S(1)}, u32[]{:S(2)}, u32[]{:S(2)}) async-start(s32[8,1,256]{2,1,0:T(1,128)} %reshape.173), calls=%async_computation.1 | async-start | bytes 16384 | tf_op jit(solution)/shard_map/all_to_all | solution.py:86
  93.5 43.3 %copy-start.2 = (bf16[768,1024]{1,0:T(8,128)(2,1)S(1)}, bf16[768,1024]{1,0:T(8,128)(2,1)}, u32[]{:S(2)}) copy-start(bf16[768,1024]{1,0:T(8,128)(2,1)} %param.10) | copy-start | bytes 4718596
  200.5 110.6 %all-to-all-start = ((bf16[8,8,192,384]{3,2,0,1:T(8,128)(2,1)}), bf16[8,8,192,384]{3,2,0,1:T(8,128)(2,1)}, u32[]{:S(2)}, u32[]{:S(2)}) async-start(bf16[8,8,192,384]{3,2,0,1:T(8,128)(2,1)} %copy.49), calls=%async_computation | async-start | bytes 18874368 | tf_op jit(solution)/shard_map/all_to_all | solution.py:85
  324.4 2.2 copy-start
  335.0 4.9 copy-start.3
  335.0 42.5 %all-to-all-start.2 = ((bf16[8,8,192,128]{3,2,0,1:T(8,128)(2,1)}), bf16[8,8,192,128]{3,2,0,1:T(8,128)(2,1)}, u32[]{:S(2)}, u32[]{:S(2)}) async-start(bf16[8,8,192,128]{3,2,0,1:T(8,128)(2,1)} %copy.58), calls=%async_computation.2 | async-start | bytes 6291456 | tf_op jit(solution)/shard_map/all_to_all | solution.py:89
  339.5 181.7 %all-gather.2.cloned.1.call-start = ((), (), s32[]{:S(2)}) async-start(), calls=%async_computation.3 | async-start | bytes 7864320 | tf_op jit(solution)/shard_map/all_gather | solution.py:96
  404.7 2.5 copy-start.1
  406.3 2.6 copy-start.4
Sparse Core Ops, SparseCore 0:
  406.5 114.7 all-gather.1

commit v2 on v1

--- a/solution.py
+++ b/solution.py
@@ -50,53 +50,67 @@
     return result.reshape(heads_here, sources, width_slots, head_dim), key_sums, key_counts
 
 
+GROUPS = 2
+
+
 def local(query_rows, key_rows, value_rows, cluster_ids, centroids, out_weight):
     ctx_count = lax.axis_size("ctx")
+    head_count = lax.axis_size("head")
     token_count = query_rows.shape[0]
     heads_here = cluster_ids.shape[0]
     head_dim = query_rows.shape[1] // heads_here
+    out_cols = out_weight.shape[1]
     clusters = CLUSTERS
     per_owner = clusters // ctx_count
     slot_count = 2 * token_count // clusters
     row_total = clusters * slot_count
+    groups = GROUPS if heads_here % GROUPS == 0 else 1
+    group_heads = heads_here // groups
     labels = cluster_ids[:, :, 0]
     targets = slot_targets(labels, per_owner, slot_count)
-    head_ids = jnp.arange(heads_here, dtype=jnp.int32)
-    token_ids = jnp.arange(token_count, dtype=jnp.int32)
-    token_at = jnp.full((heads_here, row_total), token_count, jnp.int32)
-    token_at = token_at.at[head_ids[:, None], targets].set(
-        jnp.broadcast_to(token_ids[None, :], targets.shape), unique_indices=True
-    )
-    filled_slot = token_at < token_count
-    flat_index = jnp.where(filled_slot, token_at * heads_here + head_ids[:, None], 0)
-
-    def pick(rows):
-        table = rows.reshape(token_count * heads_here, head_dim)
-        got = jnp.take(table, flat_index, axis=0)
-        return jnp.where(filled_slot[..., None], got, jnp.zeros_like(got))
-
-    send = jnp.concatenate(
-        (pick(query_rows), pick(key_rows), pick(value_rows)), axis=2
-    ).reshape(heads_here, ctx_count, slot_count * per_owner, 3 * head_dim)
     one_hot = labels[:, :, None] == jnp.arange(clusters, dtype=jnp.int32)[None, None, :]
     counts_send = jnp.sum(one_hot.astype(jnp.int32), axis=1).reshape(
         heads_here, ctx_count, per_owner
     )
-    recv = lax.all_to_all(send, "ctx", split_axis=1, concat_axis=1, tiled=True)
     counts_recv = lax.all_to_all(counts_send, "ctx", split_axis=1, concat_axis=1, tiled=True)
-    result, key_sums, key_counts = attend_blocks(recv, counts_recv, per_owner, head_dim)
+    stacked = jnp.concatenate(
+        (
+            query_rows.reshape(token_count, heads_here, head_dim),
+            key_rows.reshape(token_count, heads_here, head_dim),
+            value_rows.reshape(token_count, heads_here, head_dim),
+        ),
+        axis=2,
+    )
+    weight_view = out_weight.reshape(head_count, groups, group_heads * head_dim, out_cols)
+    slot_ids = jnp.arange(row_total, dtype=jnp.int32)
+    mixed_total = None
+    sums_parts, counts_parts = [], []
+    for g in range(groups):
+        heads = slice(g * group_heads, (g + 1) * group_heads)
+        selector = (slot_ids[None, :, None] == targets[heads][:, None, :]).astype(jnp.bfloat16)
+        send = jnp.einsum(
+            "hrt,thd->hrd", selector, stacked[:, heads], preferred_element_type=jnp.float32
+        ).astype(jnp.bfloat16)
+        send = send.reshape(group_heads, ctx_count, slot_count * per_owner, 3 * head_dim)
+        recv = lax.all_to_all(send, "ctx", split_axis=1, concat_axis=1, tiled=True)
+        result, key_sums, key_counts = attend_blocks(recv, counts_recv[heads], per_owner, head_dim)
+        sums_parts.append(key_sums)
+        counts_parts.append(key_counts)
+        returned = lax.all_to_all(result, "ctx", split_axis=1, concat_axis=1, tiled=True)
+        returned = returned.reshape(group_heads, row_total, head_dim)
+        attended = jnp.einsum(
+            "hrt,hrd->thd", selector, returned, preferred_element_type=jnp.float32
+        ).astype(jnp.bfloat16).reshape(token_count, group_heads * head_dim)
+        gathered = lax.all_gather(attended, "head", axis=1, tiled=True)
+        part = jnp.dot(
+            gathered,
+            weight_view[:, g].reshape(head_count * group_heads * head_dim, out_cols),
+            preferred_element_type=jnp.float32,
+        )
+        mixed_total = part if mixed_total is None else mixed_total + part
+    key_sums = jnp.concatenate(sums_parts, axis=0)
+    key_counts = jnp.concatenate(counts_parts, axis=0)
     new_centroids = (prior_weight * centroids + key_sums) / (prior_weight + key_counts[:, :, None])
-    returned = lax.all_to_all(result, "ctx", split_axis=1, concat_axis=1, tiled=True)
-    returned_flat = returned.reshape(heads_here * row_total, head_dim)
-    back_index = jnp.transpose(targets + head_ids[:, None] * row_total, (1, 0))
-    attended = jnp.take(returned_flat, back_index, axis=0).reshape(
-        token_count, heads_here * head_dim
-    )
-    mixed_total = jnp.dot(
-        lax.all_gather(attended, "head", axis=1, tiled=True),
-        out_weight,
-        preferred_element_type=jnp.float32,
-    )
     return (mixed_total.astype(jnp.bfloat16), new_centroids)
 
 

time: 541 us -> 321 us (0.59)
  local copies, waits for them, and re-layouts: 213 us -> 39.4 us
  waiting for transfers between devices: 252 us -> 162 us
  matrix products: 16.4 us -> 50.9 us
  blocking collectives: 0 us -> 23.4 us
  other arithmetic: 28.9 us -> 11.6 us
    gather x4 -> x0, local copies, waits for them, and re-layouts: 152 us -> none  [the longest x3 130 us: pick(): got = jnp.take(table, flat_index, axis=0)]
    all_gather x1 -> x2, waiting for transfers between devices: 112 us -> 48.2 us  [local(): gathered = lax.all_gather(attended, 'head', axis=1, tiled=True)]
    all_to_all x1, waiting for transfers between devices: 36.9 us -> 11.3 us  [local(): lax.all_to_all(result, 'ctx', split_axis=1, concat_axis=1, tiled=True)]
    all_to_all x0 -> x1, blocking collectives: none -> 23.4 us  [local(): lax.all_to_all(result, 'ctx', split_axis=1, concat_axis=1, tiled=True)]
    dot_general x2 -> x6, matrix products: 14.2 us -> 35.8 us  [the longest x2 14 us: local(): jnp.dot(gathered, weight_view[:, g].reshape(head_count * group_heads * he...]
    unnamed x16 -> x10, local copies, waits for them, and re-layouts: 26.9 us -> 8.39 us
    select_n x3 -> x0, other arithmetic: 10.1 us -> none  [the longest x1 6.46 us: pick(): return jnp.where(filled_slot[..., None], got, jnp.zeros_like(got))]
    sub x0 -> x2, matrix products: none -> 8.91 us  [attend_blocks(): weights = jnp.exp(scores - top_score)]
  transfers between devices with their start and end apart: 4 -> 6, of which waited for: 3 -> 4; matrix products, arithmetic and copies ran while one was open for 35% -> 24% of each run, Pallas kernels for 0% -> 0%
where the time goes in v2:
time: 321 us; the launch traced here: 320 us
  waiting for transfers between devices  162 us (50%)
  matrix products  50.9 us (16%)
  local copies, waits for them, and re-layouts  39.4 us (12%)
  blocking collectives  23.4 us (7%)
  starting transfers between devices  18.2 us (6%)
  between operations  14.3 us (4%)
  other arithmetic  11.6 us (4%)
    all_to_all x2, waiting for transfers between devices, local(): recv = lax.all_to_all(send, 'ctx', split_axis=1, concat_axis=1, tiled=True)  103 us
    all_gather x2, waiting for transfers between devices, local(): gathered = lax.all_gather(attended, 'head', axis=1, tiled=True)  48.2 us
    all_to_all x1, blocking collectives, local(): lax.all_to_all(result, 'ctx', split_axis=1, concat_axis=1, tiled=True)  23.4 us
    dot_general x2, matrix products, local(): jnp.dot(gathered, weight_view[:, g].reshape(head_count * group_heads * he...  14 us
    dot_general x2, matrix products, local(): jnp.einsum('hrt,thd->hrd', selector, stacked[:, heads], preferred_element...  12.2 us
    all_to_all x1, waiting for transfers between devices, local(): lax.all_to_all(result, 'ctx', split_axis=1, concat_axis=1, tiled=True)  11.3 us
    dot_general x2, matrix products, local(): jnp.einsum('hrt,hrd->thd', selector, returned, preferred_element_type=jnp...  9.56 us
    all_to_all x2, starting transfers between devices, local(): recv = lax.all_to_all(send, 'ctx', split_axis=1, concat_axis=1, tiled=True)  9.21 us
  transfers between devices with their start and end apart: 6, of which 4 were waited for; matrix products, arithmetic and copies ran while one was open for 24% of the time, Pallas kernels for 0%

profile of v2, /device:TPU:0, one launch (start us, length us, event | category | flops | bytes accessed | tf_op | source)
XLA Modules:
  0.0 320.2 jit_solution(2932333089981027680)
XLA Ops:
  9.8 5.2 %all-to-all-start.1 = ((s32[8,1,256]{2,1,0:T(1,128)}), s32[8,1,256]{2,1,0:T(1,128)S(1)}, u32[]{:S(2)}, u32[]{:S(2)}) async-start(s32[8,1,256]{2,1,0:T(1,128)} %reshape.119), calls=%async_computation.1 | async-start | bytes 16384 | tf_op jit(solution)/shard_map/all_to_all | solution.py:75
  15.2 4.4 %convert_reduce_fusion = s32[8,768]{1,0:T(8,128)S(1)} fusion(s32[8,768]{1,0:T(8,128)S(1)} %bitcast.62, pred[768,768]{1,0:T(8,128)(4,1)S(1)} %iota_compare_fusion.11), kind=kLoop, calls=%fused_computation.5 | loop fusion | flops 18868224 | bytes 638976 | tf_op jit(solution)/shard_map/reduce_sum | solution.py:17
  23.0 2.6 copy.62
  25.6 1.9 copy.65
  27.5 2.6 copy.63
  30.1 2.6 copy.66
  32.7 1.8 pad_maximum_fusion
  34.5 5.3 %fusion.10 = bf16[4,1536,384]{2,1,0:T(8,128)(2,1)S(1)} fusion(s32[4,768]{1,0:T(4,128)S(1)} %get-tuple-element.15, bf16[768,8,384]{2,0,1:T(8,128)(2,1)S(1)} %pad_maximum_fusion), kind=kOutput, calls=%fused_computation.16 | convolution fusion | flops 3630956544 | bytes 7090176 | tf_op jit(solution)/shard_map/hrt,thd->hrd/dot_general | solution.py:91
  39.8 2.8 copy.67
  42.6 4.6 %all-to-all-start = ((bf16[4,8,192,384]{3,2,0,1:T(8,128)(2,1)}), bf16[4,8,192,384]{3,2,0,1:T(8,128)(2,1)}, u32[]{:S(2)}, u32[]{:S(2)}) async-start(bf16[4,8,192,384]{3,2,0,1:T(8,128)(2,1)} %copy.67), calls=%async_computation | async-start | bytes 9437184 | tf_op jit(solution)/shard_map/all_to_all | solution.py:95
  48.8 53.2 %all-to-all-done = bf16[4,8,192,384]{3,2,0,1:T(8,128)(2,1)} async-done(((bf16[4,8,192,384]{3,2,0,1:T(8,128)(2,1)}), bf16[4,8,192,384]{3,2,0,1:T(8,128)(2,1)}, u32[]{:S(2)}, u32[]{:S(2)}) %all-to-all-start) | async-done | bytes 4718624 | tf_op jit(solution)/shard_map/all_to_all | solution.py:95
  102.0 2.8 copy.68
  104.8 2.3 fusion.56
  107.1 4.4 %fusion.58 = (f32[4,32,48]{2,1,0:T(8,128)S(1)}, f32[4,32,48,48]{2,3,1,0:T(8,128)}) fusion(pred[48,48]{0,1:T(8,128)(4,1)S(1)} %iota_compare_fusion.16, pred[4,32,48]{2,1,0:T(8,128)(4,1)S(1)} %copy.71, bf16[4,48,32,128]{3,2,1,0:T(8,128)(2,1)} %get-tuple-element.10, bf16[4,48,32,128]{3,2,1,0:T(8,128)(2,1)S(1)} %get-tuple-element.11), kind=kOutput, calls=%fused_computation.86 | convolution fusion | flops 76972080 | bytes 4358400 | tf_op jit(solution)/shard_map/sub | solution.py:42
  111.5 2.9 fusion.32
  116.1 3.8 %all-to-all-start.2 = ((bf16[4,8,192,128]{3,2,0,1:T(8,128)(2,1)}), bf16[4,8,192,128]{3,2,0,1:T(8,128)(2,1)S(1)}, u32[]{:S(2)}, u32[]{:S(2)}) async-start(bf16[4,8,192,128]{3,2,0,1:T(8,128)(2,1)} %copy.76), calls=%async_computation.2 | async-start | bytes 3145728 | tf_op jit(solution)/shard_map/all_to_all | solution.py:99
  119.9 6.9 %fusion.11 = bf16[4,1536,384]{2,1,0:T(8,128)(2,1)S(1)} fusion(s32[4,768]{1,0:T(4,128)S(1)} %get-tuple-element.14, bf16[768,8,384]{2,0,1:T(8,128)(2,1)} %copy-done), kind=kOutput, calls=%fused_computation.17 | convolution fusion | flops 3630956544 | bytes 7090176 | tf_op jit(solution)/shard_map/hrt,thd->hrd/dot_general | solution.py:91
  126.8 2.7 copy.79
  129.6 11.3 %all-to-all-done.2 = bf16[4,8,192,128]{3,2,0,1:T(8,128)(2,1)S(1)} async-done(((bf16[4,8,192,128]{3,2,0,1:T(8,128)(2,1)}), bf16[4,8,192,128]{3,2,0,1:T(8,128)(2,1)S(1)}, u32[]{:S(2)}, u32[]{:S(2)}) %all-to-all-start.2) | async-done | bytes 1572896 | tf_op jit(solution)/shard_map/all_to_all | solution.py:99
  140.9 4.6 %all-to-all-start.3 = ((bf16[4,8,192,384]{3,2,0,1:T(8,128)(2,1)}), bf16[4,8,192,384]{3,2,0,1:T(8,128)(2,1)}, u32[]{:S(2)}, u32[]{:S(2)}) async-start(bf16[4,8,192,384]{3,2,0,1:T(8,128)(2,1)} %copy.79), calls=%async_computation.3 | async-start | bytes 9437184 | tf_op jit(solution)/shard_map/all_to_all | solution.py:95
  145.6 4.8 %fusion.38 = bf16[4,128,768]{2,1,0:T(8,128)(2,1)} fusion(bf16[4,1536,128]{2,1,0:T(8,128)(2,1)S(1)} %bitcast.57, s32[4,768]{1,0:T(4,128)S(1)} %get-tuple-element.15), kind=kOutput, calls=%fused_computation.52 | convolution fusion | flops 1213071360 | bytes 2371584 | tf_op jit(solution)/shard_map/hrt,hrd->thd/dot_general | solution.py:101
  150.6 49.6 %all-to-all-done.3 = bf16[4,8,192,384]{3,2,0,1:T(8,128)(2,1)} async-done(((bf16[4,8,192,384]{3,2,0,1:T(8,128)(2,1)}), bf16[4,8,192,384]{3,2,0,1:T(8,128)(2,1)}, u32[]{:S(2)}, u32[]{:S(2)}) %all-to-all-start.3) | async-done | bytes 4718624 | tf_op jit(solution)/shard_map/all_to_all | solution.py:95
  200.2 2.8 copy.80
  203.1 2.8 fusion.55
  205.9 4.5 %fusion.59 = (f32[4,32,48]{2,1,0:T(8,128)S(1)}, f32[4,32,48,48]{2,3,1,0:T(8,128)}) fusion(pred[4,32,48]{2,1,0:T(8,128)(4,1)S(1)} %copy.82, pred[48,48]{0,1:T(8,128)(4,1)S(1)} %iota_compare_fusion.16, bf16[4,48,32,128]{3,2,1,0:T(8,128)(2,1)} %get-tuple-element.7, bf16[4,48,32,128]{3,2,1,0:T(8,128)(2,1)S(1)} %get-tuple-element.8), kind=kOutput, calls=%fused_computation.87 | convolution fusion | flops 76972080 | bytes 4358400 | tf_op jit(solution)/shard_map/sub | solution.py:42
  210.3 3.4 %fusion.35 = bf16[4,48,32,128]{3,1,2,0:T(8,128)(2,1)S(1)} fusion(f32[4,32,48,48]{2,3,1,0:T(8,128)} %get-tuple-element.21, f32[4,32,48]{2,1,0:T(8,128)S(1)} %get-tuple-element.20, bf16[4,48,32,128]{3,2,1,0:T(8,128)(2,1)} %get-tuple-element.6), kind=kOutput, calls=%fused_computation.51 | convolution fusion | flops 76873728 | bytes 4349952 | tf_op jit(solution)/shard_map/hcij,hjcd->hicd/dot_general | solution.py:45
  214.3 23.4 %all_to_all.25 = bf16[4,8,192,128]{3,2,0,1:T(8,128)(2,1)S(1)} all-to-all(bf16[4,8,192,128]{3,2,0,1:T(8,128)(2,1)S(1)} %copy.87), channel_id=1, replica_groups=mesh['ctx'=8,'head'=4] {'ctx'}, dimensions={1} | all-to-all | bytes 3145728 | tf_op jit(solution)/shard_map/all_to_all | solution.py:99
  237.8 4.8 %fusion.39 = bf16[4,128,768]{2,1,0:T(8,128)(2,1)} fusion(bf16[4,1536,128]{2,1,0:T(8,128)(2,1)S(1)} %bitcast.58, s32[4,768]{1,0:T(4,128)S(1)} %get-tuple-element.14), kind=kOutput, calls=%fused_computation.53 | convolution fusion | flops 1213071360 | bytes 2371584 | tf_op jit(solution)/shard_map/hrt,hrd->thd/dot_general | solution.py:101
  242.6 6.0 %fusion.54 = (bf16[4,1,512,1024]{3,2,1,0:T(8,128)(2,1)}, bf16[4,1,512,1024]{3,2,1,0:T(8,128)(2,1)}) fusion(bf16[4,2,512,1024]{3,2,1,0:T(8,128)(2,1)} %bitcast.47), kind=kLoop, calls=%fused_computation.82 | loop fusion | bytes 16777216 | tf_op jit(solution)/shard_map/slice | solution.py:107
  251.1 6.3 %fusion.76 = f32[768,1024]{1,0:T(8,128)S(1)} fusion(bf16[768,2048]{0,1:T(8,128)(2,1)} %all-gather.3.cloned.1.call-done, bf16[2048,1024]{1,0:T(8,128)(2,1)} %bitcast.56), kind=kOutput, calls=%fused_computation.89 | convolution fusion | flops 3221225472 | bytes 10485760 | tf_op jit(solution)/shard_map/dot_general | solution.py:105
  257.4 48.2 %all-gather.5.cloned.1.call-done = bf16[768,2048]{0,1:T(8,128)(2,1)} async-done(((bf16[768,512]{0,1:T(8,128)(2,1)}), bf16[768,2048]{0,1:T(8,128)(2,1)}) %all-gather.5.cloned.1.call-update) | async-done | bytes 3145744 | tf_op jit(solution)/shard_map/all_gather | solution.py:104
  305.6 7.8 %add_convert_fusion = bf16[768,1024]{1,0:T(8,128)(2,1)} fusion(f32[768,1024]{1,0:T(8,128)S(1)} %fusion.76, bf16[768,2048]{0,1:T(8,128)(2,1)} %all-gather.5.cloned.1.call-done, bf16[2048,1024]{1,0:T(8,128)(2,1)} %bitcast.55), kind=kOutput, calls=%fused_computation.20 | convolution fusion | flops 3222798336 | bytes 12058624 | tf_op jit(solution)/shard_map/dot_general | solution.py:105
  (41 shorter events, 13.0 us)
Async XLA Ops:
  9.8 32.7 %all-to-all-start.1 = ((s32[8,1,256]{2,1,0:T(1,128)}), s32[8,1,256]{2,1,0:T(1,128)S(1)}, u32[]{:S(2)}, u32[]{:S(2)}) async-start(s32[8,1,256]{2,1,0:T(1,128)} %reshape.119), calls=%async_computation.1 | async-start | bytes 16384 | tf_op jit(solution)/shard_map/all_to_all | solution.py:75
  34.5 5.3 %copy-start = (bf16[768,8,384]{2,0,1:T(8,128)(2,1)}, bf16[768,8,384]{2,0,1:T(8,128)(2,1)S(1)}, u32[]{:S(2)}) copy-start(bf16[768,8,384]{2,0,1:T(8,128)(2,1)S(1)} %pad_maximum_fusion) | copy-start | bytes 14155780
  42.6 59.4 %all-to-all-start = ((bf16[4,8,192,384]{3,2,0,1:T(8,128)(2,1)}), bf16[4,8,192,384]{3,2,0,1:T(8,128)(2,1)}, u32[]{:S(2)}, u32[]{:S(2)}) async-start(bf16[4,8,192,384]{3,2,0,1:T(8,128)(2,1)} %copy.67), calls=%async_computation | async-start | bytes 9437184 | tf_op jit(solution)/shard_map/all_to_all | solution.py:95
  116.1 24.7 %all-to-all-start.2 = ((bf16[4,8,192,128]{3,2,0,1:T(8,128)(2,1)}), bf16[4,8,192,128]{3,2,0,1:T(8,128)(2,1)S(1)}, u32[]{:S(2)}, u32[]{:S(2)}) async-start(bf16[4,8,192,128]{3,2,0,1:T(8,128)(2,1)} %copy.76), calls=%async_computation.2 | async-start | bytes 3145728 | tf_op jit(solution)/shard_map/all_to_all | solution.py:99
  140.9 59.3 %all-to-all-start.3 = ((bf16[4,8,192,384]{3,2,0,1:T(8,128)(2,1)}), bf16[4,8,192,384]{3,2,0,1:T(8,128)(2,1)}, u32[]{:S(2)}, u32[]{:S(2)}) async-start(bf16[4,8,192,384]{3,2,0,1:T(8,128)(2,1)} %copy.79), calls=%async_computation.3 | async-start | bytes 9437184 | tf_op jit(solution)/shard_map/all_to_all | solution.py:95
  145.5 105.7 %all-gather.3.cloned.1.call-start = ((), (), s32[]{:S(2)}) async-start(), calls=%async_computation.5 | async-start | bytes 3932160 | tf_op jit(solution)/shard_map/all_gather | solution.py:104
  150.4 155.2 %all-gather.5.cloned.1.call-start = ((), (), s32[]{:S(2)}) async-start(), calls=%async_computation.6 | async-start | bytes 3932160 | tf_op jit(solution)/shard_map/all_gather | solution.py:104
  248.6 1.8 copy-start.1
Sparse Core Ops, SparseCore 0:
  150.6 65.0 all-gather.2
  242.7 62.8 all-gather.4
